TPU v7x, 32 devices: a whole 2x2x4 slice. The times are simulated.
32 devices in a mesh: groups: 2 (over x), wide: 16 (over z, y, core).
Axes of the slice: x: 2, y: 2, z: 4, core: 2. Of those that a mesh axis runs over, the one named last changes fastest.
Arguments:
- query_act: bfloat16 [4096, 2048], P(('groups', 'wide')), parts along dimension 0, may hold values from -6 to 6
- query_grad: bfloat16 [4096, 4096], P(('groups', 'wide')), parts along dimension 0, may hold values from -6 to 6
- query_positions: int32 [4096], P(('groups', 'wide')), parts along dimension 0, may hold values from 0 to 4095
- act_basis: bfloat16 [2048, 1024], P(None, 'wide'), may hold values from -0.125 to 0.125
- grad_basis: bfloat16 [4096, 2048], P(None, 'wide'), may hold values from -0.09375 to 0.09375
- eig_values: bfloat16 [1024, 2048], P('wide'), may hold values from 0.05 to 50, as said below
- damping_index: int32 [12], P('groups'), parts along dimension 0, may hold values from 0 to 8
- train_act_rot: bfloat16 [1024, 6144], P(None, 'wide'), may hold values from -6 to 6
- train_grad_rot: bfloat16 [2048, 6144], P(None, 'wide'), may hold values from -6 to 6
- train_positions: int32 [6144], P('wide'), may hold values from 0 to 4095
Outputs:
- influences: float32 [12, 6144], P('groups', 'wide'), parts along dimension 0
There are 2 independent parts, one for each index of `groups`. A program takes and returns all parts, laid end to end along the dimension named above; an argument that names none is the same for every part. Nothing has to cross between parts.
Inputs may be any that keep to these rules, and one draw needn't show every extreme that they name: `eig_values`: positive corrected eigenvalues.
All inputs are finite; a program needn't handle non-finite values.
Results may differ from a plain program's by a relative error of at most 0.0059.
Values may be sent and summed in bfloat16 or wider, within the bound.
No kernel may reach another device: no remote copies, remote signals or barrier semaphores. Data moves between devices by JAX's collectives and lax.ppermute only.
A program may use at most 128 MiB of HBM per device.

v0:
```python
import math
import jax
import jax.numpy as jnp
from jax import lax
from jax.sharding import PartitionSpec as P

EIG_IN = 1024
EIG_OUT = 2048
PROMPT = 1024


def score_rows(grad_rows, eig_rows, dampings, train_act_rot, train_grad_rot):
    acts_rows = train_act_rot.astype(jnp.float32)
    grad_wide = grad_rows.astype(jnp.float32)
    eig_wide = eig_rows.astype(jnp.float32)
    results = []
    for damping in range(dampings.shape[0]):
        precond = (grad_wide / (eig_wide + dampings[damping])).astype(jnp.bfloat16)
        projected = jnp.dot(precond, train_grad_rot, preferred_element_type=jnp.float32)
        results.append(jnp.sum(projected * acts_rows, axis=0))
    return jnp.stack(results)


def shards(
    query_act,
    query_grad,
    query_positions,
    act_basis,
    grad_basis,
    eig_values,
    damping_index,
    train_act_rot,
    train_grad_rot,
    train_positions,
):
    act_full = jnp.dot(
        query_act,
        lax.all_gather(act_basis, "wide", axis=1, tiled=True),
        preferred_element_type=jnp.float32,
    )
    grad_full = jnp.dot(
        query_grad,
        lax.all_gather(grad_basis, "wide", axis=1, tiled=True),
        preferred_element_type=jnp.float32,
    )
    act_rot = act_full.astype(jnp.bfloat16)
    grad_rot = grad_full.astype(jnp.bfloat16)
    query_weight = jnp.where(query_positions >= PROMPT, 1.0, 0.0).astype(jnp.bfloat16)
    grad_kept = grad_rot * query_weight[:, None]
    eig_total = lax.psum(jnp.sum(eig_values.astype(jnp.float32)), "wide")
    mean_eig = eig_total / (EIG_IN * EIG_OUT)
    dampings = mean_eig * jnp.exp2(damping_index.astype(jnp.float32) - 4.0)
    partial_whole = lax.dot_general(
        act_rot, grad_kept, (((0,), (0,)), ((), ())), preferred_element_type=jnp.float32
    )
    query_gradient = lax.psum(partial_whole, "wide").astype(jnp.bfloat16)
    totals = score_rows(
        query_gradient,
        lax.all_gather(eig_values, "wide", axis=0, tiled=True),
        dampings,
        train_act_rot,
        train_grad_rot,
    )
    query_count = query_act.shape[0] * lax.axis_size("wide")
    factor = mean_eig * (1.0 / math.sqrt(float(query_count) * EIG_IN * EIG_OUT))
    train_weight = jnp.where(train_positions >= PROMPT, 1.0, 0.0).astype(jnp.float32)
    return totals * factor * train_weight[None, :]


def solution(mesh):
    in_specs = (
        P(("groups", "wide"), None),
        P(("groups", "wide"), None),
        P(("groups", "wide")),
        P(None, "wide"),
        P(None, "wide"),
        P("wide", None),
        P("groups"),
        P(None, "wide"),
        P(None, "wide"),
        P("wide"),
    )
    out_specs = P("groups", "wide")
    return jax.shard_map(shards, mesh=mesh, in_specs=in_specs, out_specs=out_specs, check_vma=False)
```

profile of v0, /device:TPU:1, one launch (start us, length us, event | category | flops | bytes accessed | tf_op | source)
XLA Modules:
  0.0 428.8 jit_solution(4725387925321449047)
XLA Ops:
  6.5 0.0 copy-start
  6.5 0.7 all-gather.6.cloned.1.call-update
  7.3 0.0 all-gather.4.cloned.1.call-start
  7.3 0.7 all-gather.4.cloned.1.call-update
  8.0 0.0 all-gather.8.cloned.1.call-start
  8.1 0.7 all-gather.8.cloned.1.call-update
  8.7 1.7 convert_reduce_fusion
  10.4 0.7 fusion.38
  11.1 0.7 compare_select_fusion
  11.8 130.6 %all-gather.6.cloned.1.call-done = bf16[4096,2048]{1,0:T(8,128)(2,1)} async-done(((bf16[4096,128]{1,0:T(8,128)(2,1)}), bf16[4096,2048]{1,0:T(8,128)(2,1)}) %all-gather.6.cloned.1.call-update) | async-done | bytes 16777232 | tf_op jit(solution)/shard_map/all_gather | solution.py:43
  142.4 8.4 %fusion.18 = bf16[128,2048]{1,0:T(8,128)(2,1)S(1)} fusion(bf16[128,4096]{1,0:T(8,128)(2,1)} %param.11, bf16[4096,2048]{1,0:T(8,128)(2,1)} %all-gather.6.cloned.1.call-done, bf16[128]{0:T(256)(128)(2,1)S(1)} %fusion.38), kind=kOutput, calls=%fused_computation.31 | convolution fusion | flops 2148007936 | bytes 18350336 | tf_op jit(solution)/shard_map/dot_general | solution.py:41
  150.8 42.5 %all-gather.4.cloned.1.call-done = bf16[2048,1024]{0,1:T(8,128)(2,1)} async-done(((bf16[2048,64]{0,1:T(8,128)(2,1)}), bf16[2048,1024]{0,1:T(8,128)(2,1)}) %all-gather.4.cloned.1.call-update) | async-done | bytes 4194320 | tf_op jit(solution)/shard_map/all_gather | solution.py:38
  193.3 0.0 copy-done.1
  193.3 8.1 %fusion.37 = f32[1024,2048]{1,0:T(8,128)} fusion(bf16[128,2048]{1,0:T(8,128)(2,1)S(1)} %fusion.18, bf16[128,2048]{1,0:T(8,128)(2,1)S(1)} %copy-done.1, bf16[2048,1024]{0,1:T(8,128)(2,1)} %all-gather.4.cloned.1.call-done), kind=kOutput, calls=%fused_computation.39 | convolution fusion | flops 1073872896 | bytes 13631488 | tf_op jit(solution)/shard_map/dot_general | solution.py:53
  201.4 195.6 %all-reduce.2 = (bf16[1024,2048]{1,0:T(8,128)(2,1)}, f32[]{:T(128)}) all-reduce(f32[1024,2048]{1,0:T(8,128)} %fusion.37, f32[]{:T(128)} %convert_reduce_fusion), channel_id=1, replica_groups=mesh['groups'=2,'wide'=16] {'wide'}, use_global_device_ids=true, to_apply=%region_0.1 | all-reduce | flops 2097153 | bytes 12582920 | tf_op jit(solution)/shard_map/psum | solution.py:56
  397.8 0.7 fusion.39
  398.4 0.0 copy-done.4
  398.5 7.0 %fusion.24 = f32[384]{0:T(512)S(1)} fusion(bf16[1024,384]{1,0:T(8,128)(2,1)S(1)} %copy-done.4, bf16[2048,384]{1,0:T(8,128)(2,1)S(1)} %copy-done, bf16[1024,2048]{1,0:T(8,128)(2,1)} %get-tuple-element.5, bf16[1024,2048]{1,0:T(8,128)(2,1)} %all-gather.8.cloned.1.call-done, f32[]{:T(128)} %bitcast.5), kind=kOutput, calls=%fused_computation.37 | convolution fusion | flops 1622277760 | bytes 10749444 | tf_op jit(solution)/shard_map/dot_general | solution.py:19
  405.5 3.0 fusion.23
  408.5 3.1 fusion.22
  411.6 3.0 fusion.21
  414.6 3.3 fusion.20
  417.9 3.0 fusion.19
  421.6 0.6 multiply_multiply_fusion
  (19 shorter events, 0.1 us)
Async XLA Ops:
  6.5 391.9 %copy-start = (bf16[2048,384]{1,0:T(8,128)(2,1)S(1)}, bf16[2048,384]{1,0:T(8,128)(2,1)}, u32[]{:S(2)}) copy-start(bf16[2048,384]{1,0:T(8,128)(2,1)} %param.18) | copy-start | bytes 4718596
  6.5 135.9 %all-gather.6.cloned.1.call-start = ((), (), s32[]{:S(2)}) async-start(), calls=%async_computation.1 | async-start | bytes 17825792 | tf_op jit(solution)/shard_map/all_gather | solution.py:43
  7.3 186.1 %all-gather.4.cloned.1.call-start = ((), (), s32[]{:S(2)}) async-start(), calls=%async_computation | async-start | bytes 4456448 | tf_op jit(solution)/shard_map/all_gather | solution.py:38
  8.0 390.4 %all-gather.8.cloned.1.call-start = ((), (), s32[]{:S(2)}) async-start(), calls=%async_computation.2 | async-start | bytes 4456448 | tf_op jit(solution)/shard_map/all_gather | solution.py:59
  11.8 181.6 %copy-start.1 = (bf16[128,2048]{1,0:T(8,128)(2,1)S(1)}, bf16[128,2048]{1,0:T(8,128)(2,1)}, u32[]{:S(2)}) copy-start(bf16[128,2048]{1,0:T(8,128)(2,1)} %param.10) | copy-start | bytes 1572868
  201.4 196.3 %copy-start.5 = (s32[6]{0:T(128)S(1)}, s32[6]{0:T(128)}, u32[]{:S(2)}) copy-start(s32[6]{0:T(128)} %param.16) | copy-start | bytes 76
  201.4 197.0 %copy-start.4 = (bf16[1024,384]{1,0:T(8,128)(2,1)S(1)}, bf16[1024,384]{1,0:T(8,128)(2,1)}, u32[]{:S(2)}) copy-start(bf16[1024,384]{1,0:T(8,128)(2,1)} %param.17) | copy-start | bytes 2359300
  398.4 7.0 %copy-start.2 = (bf16[1024,2048]{1,0:T(8,128)(2,1)S(1)}, bf16[1024,2048]{1,0:T(8,128)(2,1)}, u32[]{:S(2)}) copy-start(bf16[1024,2048]{1,0:T(8,128)(2,1)} %all-gather.8.cloned.1.call-done) | copy-start | bytes 12582916
  398.4 7.0 %copy-start.3 = (bf16[1024,2048]{1,0:T(8,128)(2,1)S(1)}, bf16[1024,2048]{1,0:T(8,128)(2,1)}, u32[]{:S(2)}) copy-start(bf16[1024,2048]{1,0:T(8,128)(2,1)} %get-tuple-element.5) | copy-start | bytes 12582916
Sparse Core Ops, SparseCore 0:
  9.5 132.8 all-gather.5
  144.6 48.7 all-gather.3
  195.5 67.8 all-gather.7
where the time goes:
time: 429 us
  blocking collectives  196 us (46%)
  waiting for transfers between devices  175 us (41%)
  matrix products  39 us (9%)
  between operations  14.5 us (3%)
    psum x1, blocking collectives, shards(): query_gradient = lax.psum(partial_whole, 'wide').astype(jnp.bfloat16)  196 us
    all_gather x1, waiting for transfers between devices, shards(): lax.all_gather(grad_basis, 'wide', axis=1, tiled=True)  131 us
    all_gather x1, waiting for transfers between devices, shards(): lax.all_gather(act_basis, 'wide', axis=1, tiled=True)  42.5 us
    dot_general x6, matrix products, score_rows(): jnp.dot(precond, train_grad_rot, preferred_element_type=jnp.float32)  22.4 us
  transfers between devices with their start and end apart: 3, of which 2 were waited for; matrix products, arithmetic and copies ran while one was open for 5% of the time, Pallas kernels for 0%

commit v1 on v0

--- a/solution.py
+++ b/solution.py
@@ -7,6 +7,24 @@
 EIG_IN = 1024
 EIG_OUT = 2048
 PROMPT = 1024
+
+
+def collect(value, axis, dim):
+    ways, here, step = (lax.axis_size(axis), lax.axis_index(axis), value.shape[dim])
+    dims = [n * ways if d == dim else n for d, n in enumerate(value.shape)]
+    full = lax.dynamic_update_slice_in_dim(
+        jnp.zeros(dims, value.dtype), value, here * step, axis=dim
+    )
+    going_up = going_down = value
+    for far in range(1, ways // 2 + 1):
+        going_up = lax.ppermute(going_up, axis, [(d, (d + 1) % ways) for d in range(ways)])
+        full = lax.dynamic_update_slice_in_dim(full, going_up, (here - far) % ways * step, axis=dim)
+        if 2 * far < ways:
+            going_down = lax.ppermute(going_down, axis, [(d, (d - 1) % ways) for d in range(ways)])
+            full = lax.dynamic_update_slice_in_dim(
+                full, going_down, (here + far) % ways * step, axis=dim
+            )
+    return full
 
 
 def score_rows(grad_rows, eig_rows, dampings, train_act_rot, train_grad_rot):
@@ -39,9 +57,7 @@
         preferred_element_type=jnp.float32,
     )
     grad_full = jnp.dot(
-        query_grad,
-        lax.all_gather(grad_basis, "wide", axis=1, tiled=True),
-        preferred_element_type=jnp.float32,
+        query_grad, collect(grad_basis, "wide", 1), preferred_element_type=jnp.float32
     )
     act_rot = act_full.astype(jnp.bfloat16)
     grad_rot = grad_full.astype(jnp.bfloat16)

time: 429 us -> 462 us (1.077)
  local copies, waits for them, and re-layouts: 0.75 us -> 32.1 us
  starting transfers between devices: 0.08 us -> 20.1 us
  blocking collectives: 196 us -> 185 us
  waiting for transfers between devices: 175 us -> 164 us
    ppermute x0 -> x15, waiting for transfers between devices: none -> 164 us  [the longest x8 102 us: collect(): lax.ppermute(going_up, axis, [(d, (d + 1) % ways) for d in range(ways)])]
    all_gather x1 -> x0, waiting for transfers between devices: 131 us -> none  [shards(): lax.all_gather(grad_basis, 'wide', axis=1, tiled=True)]
    all_gather x1, waiting for transfers between devices: 42.5 us -> 0.01 us  [shards(): lax.all_gather(act_basis, 'wide', axis=1, tiled=True)]
    dynamic_update_slice x0 -> x16, local copies, waits for them, and re-layouts: none -> 25.4 us  [the longest x8 15.1 us: collect(): lax.dynamic_update_slice_in_dim(full, going_up, (here - far) % ways * ste...]
    ppermute x0 -> x15, starting transfers between devices: none -> 20.1 us  [the longest x8 20 us: collect(): lax.ppermute(going_up, axis, [(d, (d + 1) % ways) for d in range(ways)])]
    psum x1, blocking collectives: 196 us -> 185 us  [shards(): query_gradient = lax.psum(partial_whole, 'wide').astype(jnp.bfloat16)]
    broadcast_in_dim x0 -> x1, local copies, waits for them, and re-layouts: none -> 5.98 us  [collect(): jnp.zeros(dims, value.dtype)]
    dot_general x1, matrix products: 8.11 us -> 13.1 us  [shards(): lax.dot_general(act_rot, grad_kept, (((0,), (0,)), ((), ())), preferred_e...]
  transfers between devices with their start and end apart: 3 -> 17, of which waited for: 2 -> 14; matrix products, arithmetic and copies ran while one was open for 5% -> 11% of each run, Pallas kernels for 0% -> 0%
where the time goes in v1:
time: 462 us; the launch traced here: 459 us
  blocking collectives  185 us (40%)
  waiting for transfers between devices  164 us (35%)
  matrix products  39 us (8%)
  local copies, waits for them, and re-layouts  32.1 us (7%)
  starting transfers between devices  20.1 us (4%)
  between operations  15.1 us (3%)
    psum x1, blocking collectives, shards(): query_gradient = lax.psum(partial_whole, 'wide').astype(jnp.bfloat16)  185 us
    ppermute x8, waiting for transfers between devices, collect(): lax.ppermute(going_up, axis, [(d, (d + 1) % ways) for d in range(ways)])  102 us
    ppermute x7, waiting for transfers between devices, collect(): lax.ppermute(going_down, axis, [(d, (d - 1) % ways) for d in range(ways)])  62.1 us
    dot_general x6, matrix products, score_rows(): jnp.dot(precond, train_grad_rot, preferred_element_type=jnp.float32)  22.1 us
    ppermute x8, starting transfers between devices, collect(): lax.ppermute(going_up, axis, [(d, (d + 1) % ways) for d in range(ways)])  20 us
    dynamic_update_slice x8, local copies, waits for them, and re-layouts, collect(): lax.dynamic_update_slice_in_dim(full, going_up, (here - far) % ways * ste...  15.1 us
    dot_general x1, matrix products, shards(): lax.dot_general(act_rot, grad_kept, (((0,), (0,)), ((), ())), preferred_e...  13.1 us
  transfers between devices with their start and end apart: 17, of which 14 were waited for; matrix products, arithmetic and copies ran while one was open for 11% of the time, Pallas kernels for 0%

profile of v1, /device:TPU:1, one launch (start us, length us, event | category | flops | bytes accessed | tf_op | source)
XLA Modules:
  0.0 459.0 jit_solution(10603701614874816364)
XLA Ops:
  10.0 26.1 %collective-permute-done = bf16[4096,128]{1,0:T(8,128)(2,1)} collective-permute-done((bf16[4096,128]{1,0:T(8,128)(2,1)}, bf16[4096,128]{1,0:T(8,128)(2,1)}, u32[]{:S(2)}, u32[]{:S(2)}) %collective-permute-start) | collective-permute-done | bytes 1048608 | tf_op jit(solution)/shard_map/ppermute | solution.py:20
  38.6 11.2 %collective-permute-done.1 = bf16[4096,128]{1,0:T(8,128)(2,1)} collective-permute-done((bf16[4096,128]{1,0:T(8,128)(2,1)}, bf16[4096,128]{1,0:T(8,128)(2,1)}, u32[]{:S(2)}, u32[]{:S(2)}) %collective-permute-start.1) | collective-permute-done | bytes 1048608 | tf_op jit(solution)/shard_map/ppermute | solution.py:23
  50.1 22.3 %collective-permute-done.2 = bf16[4096,128]{1,0:T(8,128)(2,1)} collective-permute-done((bf16[4096,128]{1,0:T(8,128)(2,1)}, bf16[4096,128]{1,0:T(8,128)(2,1)}, u32[]{:S(2)}, u32[]{:S(2)}) %collective-permute-start.2) | collective-permute-done | bytes 1048608 | tf_op jit(solution)/shard_map/ppermute | solution.py:20
  76.2 8.8 %collective-permute-done.3 = bf16[4096,128]{1,0:T(8,128)(2,1)S(1)} collective-permute-done((bf16[4096,128]{1,0:T(8,128)(2,1)}, bf16[4096,128]{1,0:T(8,128)(2,1)S(1)}, u32[]{:S(2)}, u32[]{:S(2)}) %collective-permute-start.3) | collective-permute-done | bytes 1048608 | tf_op jit(solution)/shard_map/ppermute | solution.py:23
  86.7 6.0 %broadcast_in_dim.21 = bf16[4096,2048]{1,0:T(8,128)(2,1)} broadcast(bf16[]{:T(256)} %constant.100.clone.1), dimensions={} | broadcast | bytes 16777218 | tf_op jit(solution)/shard_map/broadcast_in_dim | solution.py:16
  93.8 4.3 collective-permute-done.4
  102.9 10.7 %collective-permute-done.5 = bf16[4096,128]{1,0:T(8,128)(2,1)S(1)} collective-permute-done((bf16[4096,128]{1,0:T(8,128)(2,1)S(1)}, bf16[4096,128]{1,0:T(8,128)(2,1)S(1)}, u32[]{:S(2)}, u32[]{:S(2)}) %collective-permute-start.5) | collective-permute-done | bytes 1048608 | tf_op jit(solution)/shard_map/ppermute | solution.py:23
  118.4 8.3 %collective-permute-done.6 = bf16[4096,128]{1,0:T(8,128)(2,1)S(1)} collective-permute-done((bf16[4096,128]{1,0:T(8,128)(2,1)}, bf16[4096,128]{1,0:T(8,128)(2,1)S(1)}, u32[]{:S(2)}, u32[]{:S(2)}) %collective-permute-start.6) | collective-permute-done | bytes 1048608 | tf_op jit(solution)/shard_map/ppermute | solution.py:20
  130.2 19.1 %collective-permute-done.7 = bf16[4096,128]{1,0:T(8,128)(2,1)S(1)} collective-permute-done((bf16[4096,128]{1,0:T(8,128)(2,1)S(1)}, bf16[4096,128]{1,0:T(8,128)(2,1)S(1)}, u32[]{:S(2)}, u32[]{:S(2)}) %collective-permute-start.7) | collective-permute-done | bytes 1048608 | tf_op jit(solution)/shard_map/ppermute | solution.py:23
  152.7 8.7 %collective-permute-done.8 = bf16[4096,128]{1,0:T(8,128)(2,1)S(1)} collective-permute-done((bf16[4096,128]{1,0:T(8,128)(2,1)S(1)}, bf16[4096,128]{1,0:T(8,128)(2,1)S(1)}, u32[]{:S(2)}, u32[]{:S(2)}) %collective-permute-start.8) | collective-permute-done | bytes 1048608 | tf_op jit(solution)/shard_map/ppermute | solution.py:20
  165.1 4.8 %collective-permute-done.9 = bf16[4096,128]{1,0:T(8,128)(2,1)S(1)} collective-permute-done((bf16[4096,128]{1,0:T(8,128)(2,1)S(1)}, bf16[4096,128]{1,0:T(8,128)(2,1)S(1)}, u32[]{:S(2)}, u32[]{:S(2)}) %collective-permute-start.9) | collective-permute-done | bytes 1048608 | tf_op jit(solution)/shard_map/ppermute | solution.py:23
  172.1 14.8 %collective-permute-done.10 = bf16[4096,128]{1,0:T(8,128)(2,1)S(1)} collective-permute-done((bf16[4096,128]{1,0:T(8,128)(2,1)S(1)}, bf16[4096,128]{1,0:T(8,128)(2,1)S(1)}, u32[]{:S(2)}, u32[]{:S(2)}) %collective-permute-start.10) | collective-permute-done | bytes 1048608 | tf_op jit(solution)/shard_map/ppermute | solution.py:20
  190.5 7.4 %collective-permute-done.11 = bf16[4096,128]{1,0:T(8,128)(2,1)S(1)} collective-permute-done((bf16[4096,128]{1,0:T(8,128)(2,1)S(1)}, bf16[4096,128]{1,0:T(8,128)(2,1)S(1)}, u32[]{:S(2)}, u32[]{:S(2)}) %collective-permute-start.11) | collective-permute-done | bytes 1048608 | tf_op jit(solution)/shard_map/ppermute | solution.py:23
  200.2 12.2 %collective-permute-done.12 = bf16[4096,128]{1,0:T(8,128)(2,1)} collective-permute-done((bf16[4096,128]{1,0:T(8,128)(2,1)S(1)}, bf16[4096,128]{1,0:T(8,128)(2,1)}, u32[]{:S(2)}, u32[]{:S(2)}) %collective-permute-start.12) | collective-permute-done | bytes 1048608 | tf_op jit(solution)/shard_map/ppermute | solution.py:20
  218.5 3.7 convolution_convert_fusion.1
  222.2 4.9 %collective-permute-done.14 = bf16[4096,128]{1,0:T(8,128)(2,1)} collective-permute-done((bf16[4096,128]{1,0:T(8,128)(2,1)}, bf16[4096,128]{1,0:T(8,128)(2,1)}, u32[]{:S(2)}, u32[]{:S(2)}) %collective-permute-start.14) | collective-permute-done | bytes 1048608 | tf_op jit(solution)/shard_map/ppermute | solution.py:20
  229.4 13.1 %fusion.37 = f32[1024,2048]{1,0:T(8,128)} fusion(bf16[128,1024]{1,0:T(8,128)(2,1)S(1)} %convolution_convert_fusion.1, bf16[4096,2048]{1,0:T(8,128)(2,1)} %constant_dynamic-update-slice_fusion, bf16[128,4096]{1,0:T(8,128)(2,1)S(1)} %copy-done.1, bf16[128]{0:T(256)(128)(2,1)S(1)} %fusion.39), kind=kOutput, calls=%fused_computation.38 | convolution fusion | flops 2684878848 | bytes 26476800 | tf_op jit(solution)/shard_map/dot_general | solution.py:69
  242.6 184.6 %all-reduce.2 = (bf16[1024,2048]{1,0:T(8,128)(2,1)}, f32[]{:T(128)}) all-reduce(f32[1024,2048]{1,0:T(8,128)} %fusion.37, f32[]{:T(128)} %convert_reduce_fusion), channel_id=1, replica_groups=mesh['groups'=2,'wide'=16] {'wide'}, use_global_device_ids=true, to_apply=%region_0.1 | all-reduce | flops 2097153 | bytes 12582920 | tf_op jit(solution)/shard_map/psum | solution.py:72
  428.6 7.1 %fusion.24 = f32[384]{0:T(512)S(1)} fusion(bf16[1024,384]{1,0:T(8,128)(2,1)S(1)} %copy-done.6, bf16[2048,384]{1,0:T(8,128)(2,1)S(1)} %copy-done, bf16[1024,2048]{1,0:T(8,128)(2,1)} %get-tuple-element.5, bf16[1024,2048]{1,0:T(8,128)(2,1)} %all-gather.5.cloned.1.call-done, f32[]{:T(128)} %bitcast.5), kind=kOutput, calls=%fused_computation.37 | convolution fusion | flops 1622277760 | bytes 10749444 | tf_op jit(solution)/shard_map/dot_general | solution.py:37
  435.7 3.0 fusion.23
  438.7 3.0 fusion.22
  441.7 2.9 fusion.21
  444.6 3.3 fusion.20
  447.9 2.9 fusion.19
  (67 shorter events, 50.6 us)
Async XLA Ops:
  6.5 422.0 %copy-start = (bf16[2048,384]{1,0:T(8,128)(2,1)S(1)}, bf16[2048,384]{1,0:T(8,128)(2,1)}, u32[]{:S(2)}) copy-start(bf16[2048,384]{1,0:T(8,128)(2,1)} %param.18) | copy-start | bytes 4718596
  6.5 211.9 %all-gather.3.cloned.1.call-start = ((), (), s32[]{:S(2)}) async-start(), calls=%async_computation | async-start | bytes 4456448 | tf_op jit(solution)/shard_map/all_gather | solution.py:56
  7.3 421.3 %all-gather.5.cloned.1.call-start = ((), (), s32[]{:S(2)}) async-start(), calls=%async_computation.1 | async-start | bytes 4456448 | tf_op jit(solution)/shard_map/all_gather | solution.py:75
  7.3 28.8 %collective-permute-start = (bf16[4096,128]{1,0:T(8,128)(2,1)}, bf16[4096,128]{1,0:T(8,128)(2,1)}, u32[]{:S(2)}, u32[]{:S(2)}) collective-permute-start(bf16[4096,128]{1,0:T(8,128)(2,1)} %param.14), channel_id=1, source_target_pairs={{0,1},{1,2},{2,3},{3,4},{4,5},{5,6},{6,7},{7,8},{8,9},{9,10},{10,1... | collective-permute-start | bytes 3145736 | tf_op jit(solution)/shard_map/ppermute | solution.py:20
  10.0 39.8 %collective-permute-start.1 = (bf16[4096,128]{1,0:T(8,128)(2,1)}, bf16[4096,128]{1,0:T(8,128)(2,1)}, u32[]{:S(2)}, u32[]{:S(2)}) collective-permute-start(bf16[4096,128]{1,0:T(8,128)(2,1)} %param.14), channel_id=1, source_target_pairs={{0,15},{1,0},{2,1},{3,2},{4,3},{5,4},{6,5},{7,6},{8,7},{9,8},{10,9... | collective-permute-start | bytes 3145736 | tf_op jit(solution)/shard_map/ppermute | solution.py:23
  36.1 36.2 %collective-permute-start.2 = (bf16[4096,128]{1,0:T(8,128)(2,1)}, bf16[4096,128]{1,0:T(8,128)(2,1)}, u32[]{:S(2)}, u32[]{:S(2)}) collective-permute-start(bf16[4096,128]{1,0:T(8,128)(2,1)} %collective-permute-done), channel_id=1, source_target_pairs={{0,1},{1,2},{2,3},{3,4},{4,5},{5,6},{6,7},{7,8},{8,9},{9,10},{10,1... | collective-permute-start | bytes 3145736 | tf_op jit(solution)/shard_map/ppermute | solution.py:20
  49.8 35.2 %collective-permute-start.3 = (bf16[4096,128]{1,0:T(8,128)(2,1)}, bf16[4096,128]{1,0:T(8,128)(2,1)S(1)}, u32[]{:S(2)}, u32[]{:S(2)}) collective-permute-start(bf16[4096,128]{1,0:T(8,128)(2,1)} %collective-permute-done.1), channel_id=1, source_target_pairs={{0,15},{1,0},{2,1},{3,2},{4,3},{5,4},{6,5},{7,6},{8,7},{9,8},{10,9... | collective-permute-start | bytes 3145736 | tf_op jit(solution)/shard_map/ppermute | solution.py:23
  72.3 25.8 %collective-permute-start.4 = (bf16[4096,128]{1,0:T(8,128)(2,1)}, bf16[4096,128]{1,0:T(8,128)(2,1)}, u32[]{:S(2)}, u32[]{:S(2)}) collective-permute-start(bf16[4096,128]{1,0:T(8,128)(2,1)} %collective-permute-done.2), channel_id=1, source_target_pairs={{0,1},{1,2},{2,3},{3,4},{4,5},{5,6},{6,7},{7,8},{8,9},{9,10},{10,1... | collective-permute-start | bytes 3145736 | tf_op jit(solution)/shard_map/ppermute | solution.py:20
  85.0 28.7 %collective-permute-start.5 = (bf16[4096,128]{1,0:T(8,128)(2,1)S(1)}, bf16[4096,128]{1,0:T(8,128)(2,1)S(1)}, u32[]{:S(2)}, u32[]{:S(2)}) collective-permute-start(bf16[4096,128]{1,0:T(8,128)(2,1)S(1)} %collective-permute-done.3), channel_id=1, source_target_pairs={{0,15},{1,0},{2,1},{3,2},{4,3},{5,4},{6,5},{7,6},{8,7},{9,8},{10,9... | collective-permute-start | bytes 3145736 | tf_op jit(solution)/shard_map/ppermute | solution.py:23
  98.1 28.6 %collective-permute-start.6 = (bf16[4096,128]{1,0:T(8,128)(2,1)}, bf16[4096,128]{1,0:T(8,128)(2,1)S(1)}, u32[]{:S(2)}, u32[]{:S(2)}) collective-permute-start(bf16[4096,128]{1,0:T(8,128)(2,1)} %collective-permute-done.4), channel_id=1, source_target_pairs={{0,1},{1,2},{2,3},{3,4},{4,5},{5,6},{6,7},{7,8},{8,9},{9,10},{10,1... | collective-permute-start | bytes 3145736 | tf_op jit(solution)/shard_map/ppermute | solution.py:20
  113.6 35.7 %collective-permute-start.7 = (bf16[4096,128]{1,0:T(8,128)(2,1)S(1)}, bf16[4096,128]{1,0:T(8,128)(2,1)S(1)}, u32[]{:S(2)}, u32[]{:S(2)}) collective-permute-start(bf16[4096,128]{1,0:T(8,128)(2,1)S(1)} %collective-permute-done.5), channel_id=1, source_target_pairs={{0,15},{1,0},{2,1},{3,2},{4,3},{5,4},{6,5},{7,6},{8,7},{9,8},{10,9... | collective-permute-start | bytes 3145736 | tf_op jit(solution)/shard_map/ppermute | solution.py:23
  126.7 34.8 %collective-permute-start.8 = (bf16[4096,128]{1,0:T(8,128)(2,1)S(1)}, bf16[4096,128]{1,0:T(8,128)(2,1)S(1)}, u32[]{:S(2)}, u32[]{:S(2)}) collective-permute-start(bf16[4096,128]{1,0:T(8,128)(2,1)S(1)} %collective-permute-done.6), channel_id=1, source_target_pairs={{0,1},{1,2},{2,3},{3,4},{4,5},{5,6},{6,7},{7,8},{8,9},{9,10},{10,1... | collective-permute-start | bytes 3145736 | tf_op jit(solution)/shard_map/ppermute | solution.py:20
  149.3 20.6 %collective-permute-start.9 = (bf16[4096,128]{1,0:T(8,128)(2,1)S(1)}, bf16[4096,128]{1,0:T(8,128)(2,1)S(1)}, u32[]{:S(2)}, u32[]{:S(2)}) collective-permute-start(bf16[4096,128]{1,0:T(8,128)(2,1)S(1)} %collective-permute-done.7), channel_id=1, source_target_pairs={{0,15},{1,0},{2,1},{3,2},{4,3},{5,4},{6,5},{7,6},{8,7},{9,8},{10,9... | collective-permute-start | bytes 3145736 | tf_op jit(solution)/shard_map/ppermute | solution.py:23
  152.7 65.7 %copy-start.3 = (bf16[128,2048]{1,0:T(8,128)(2,1)S(1)}, bf16[128,2048]{1,0:T(8,128)(2,1)}, u32[]{:S(2)}) copy-start(bf16[128,2048]{1,0:T(8,128)(2,1)} %param.10) | copy-start | bytes 1572868
  161.5 25.5 %collective-permute-start.10 = (bf16[4096,128]{1,0:T(8,128)(2,1)S(1)}, bf16[4096,128]{1,0:T(8,128)(2,1)S(1)}, u32[]{:S(2)}, u32[]{:S(2)}) collective-permute-start(bf16[4096,128]{1,0:T(8,128)(2,1)S(1)} %collective-permute-done.8), channel_id=1, source_target_pairs={{0,1},{1,2},{2,3},{3,4},{4,5},{5,6},{6,7},{7,8},{8,9},{9,10},{10,1... | collective-permute-start | bytes 3145736 | tf_op jit(solution)/shard_map/ppermute | solution.py:20
  169.9 28.1 %collective-permute-start.11 = (bf16[4096,128]{1,0:T(8,128)(2,1)S(1)}, bf16[4096,128]{1,0:T(8,128)(2,1)S(1)}, u32[]{:S(2)}, u32[]{:S(2)}) collective-permute-start(bf16[4096,128]{1,0:T(8,128)(2,1)S(1)} %collective-permute-done.9), channel_id=1, source_target_pairs={{0,15},{1,0},{2,1},{3,2},{4,3},{5,4},{6,5},{7,6},{8,7},{9,8},{10,9... | collective-permute-start | bytes 3145736 | tf_op jit(solution)/shard_map/ppermute | solution.py:23
  172.1 57.3 %copy-start.1 = (bf16[128,4096]{1,0:T(8,128)(2,1)S(1)}, bf16[128,4096]{1,0:T(8,128)(2,1)}, u32[]{:S(2)}) copy-start(bf16[128,4096]{1,0:T(8,128)(2,1)} %param.11) | copy-start | bytes 3145732
  186.9 25.5 %collective-permute-start.12 = (bf16[4096,128]{1,0:T(8,128)(2,1)S(1)}, bf16[4096,128]{1,0:T(8,128)(2,1)}, u32[]{:S(2)}, u32[]{:S(2)}) collective-permute-start(bf16[4096,128]{1,0:T(8,128)(2,1)S(1)} %collective-permute-done.10), channel_id=1, source_target_pairs={{0,1},{1,2},{2,3},{3,4},{4,5},{5,6},{6,7},{7,8},{8,9},{9,10},{10,1... | collective-permute-start | bytes 3145736 | tf_op jit(solution)/shard_map/ppermute | solution.py:20
  197.9 19.4 %collective-permute-start.13 = (bf16[4096,128]{1,0:T(8,128)(2,1)S(1)}, bf16[4096,128]{1,0:T(8,128)(2,1)S(1)}, u32[]{:S(2)}, u32[]{:S(2)}) collective-permute-start(bf16[4096,128]{1,0:T(8,128)(2,1)S(1)} %collective-permute-done.11), channel_id=1, source_target_pairs={{0,15},{1,0},{2,1},{3,2},{4,3},{5,4},{6,5},{7,6},{8,7},{9,8},{10,9... | collective-permute-start | bytes 3145736 | tf_op jit(solution)/shard_map/ppermute | solution.py:23
  212.4 14.6 %collective-permute-start.14 = (bf16[4096,128]{1,0:T(8,128)(2,1)}, bf16[4096,128]{1,0:T(8,128)(2,1)}, u32[]{:S(2)}, u32[]{:S(2)}) collective-permute-start(bf16[4096,128]{1,0:T(8,128)(2,1)} %collective-permute-done.12), channel_id=1, source_target_pairs={{0,1},{1,2},{2,3},{3,4},{4,5},{5,6},{6,7},{7,8},{8,9},{9,10},{10,1... | collective-permute-start | bytes 3145736 | tf_op jit(solution)/shard_map/ppermute | solution.py:20
  242.6 185.3 %copy-start.7 = (s32[6]{0:T(128)S(1)}, s32[6]{0:T(128)}, u32[]{:S(2)}) copy-start(s32[6]{0:T(128)} %param.16) | copy-start | bytes 76
  242.6 186.0 %copy-start.6 = (bf16[1024,384]{1,0:T(8,128)(2,1)S(1)}, bf16[1024,384]{1,0:T(8,128)(2,1)}, u32[]{:S(2)}) copy-start(bf16[1024,384]{1,0:T(8,128)(2,1)} %param.17) | copy-start | bytes 2359300
  428.6 7.1 %copy-start.4 = (bf16[1024,2048]{1,0:T(8,128)(2,1)S(1)}, bf16[1024,2048]{1,0:T(8,128)(2,1)}, u32[]{:S(2)}) copy-start(bf16[1024,2048]{1,0:T(8,128)(2,1)} %all-gather.5.cloned.1.call-done) | copy-start | bytes 12582916
  428.6 7.1 %copy-start.5 = (bf16[1024,2048]{1,0:T(8,128)(2,1)S(1)}, bf16[1024,2048]{1,0:T(8,128)(2,1)}, u32[]{:S(2)}) copy-start(bf16[1024,2048]{1,0:T(8,128)(2,1)} %get-tuple-element.5) | copy-start | bytes 12582916
  (1 other events, 6.0 us)
Sparse Core Ops, SparseCore 0:
  9.5 80.4 all-gather.2
  92.2 68.2 all-gather.4
